TPU v7x, 32 devices: a whole 2x2x4 slice. The times are simulated.
32 devices in a mesh: walk: 4 (over x, core), chol: 8 (over z, y).
Axes of the slice: x: 2, y: 2, z: 4, core: 2. Of those that a mesh axis runs over, the one named last changes fastest.
Arguments:
- old_walkers: bfloat16 [96, 2048, 128], P(('walk', 'chol'))
- half_chol: bfloat16 [16, 128, 2048], P('chol'), may hold values from -0.1875 to 0.1875
- parent: int32 [192], P(('walk', 'chol')), may hold values from -1 to 11, as said below
- field: float32 [192, 2048], P(('walk', 'chol')), may hold values from -0.8 to 0.8
Outputs:
- new_walkers: bfloat16 [192, 2048, 128], P(('walk', 'chol'))
- energy: float32 [192], P(('walk', 'chol'))
Inputs may be any that keep to these rules, and one draw needn't show every extreme that they name: `parent`: the 4 devices that share an index of chol form a column. On each device the live slots (value >= 0) come first among its 6 slots, the rest hold -1. Each column has exactly 12 live slots, every device of it at least one, and some device of it has all 6 slots live. A live value m names the walker that the column's walk index m // 3 holds as its local walker m % 3.
All inputs are finite; a program needn't handle non-finite values.
Results may differ from a plain program's by a relative error of at most 0.0062.
Values may be sent and summed in bfloat16 or wider, within the bound.
No kernel may reach another device: no remote copies, remote signals or barrier semaphores. Data moves between devices by JAX's collectives and lax.ppermute only.
A program may use at most 192 MiB of HBM per device.

v0:
```python
import jax
import jax.numpy as jnp
from jax import lax
from jax.sharding import PartitionSpec as P

ITERS = 3


def green_half(walkers):
    widened = walkers.astype(jnp.float32)
    electrons = walkers.shape[2]
    intersection = widened[:, :electrons, :]
    identity = jnp.eye(electrons, dtype=jnp.float32)
    diagonal = jnp.diagonal(intersection, axis1=1, axis2=2)
    inverse = identity[None, :, :] / diagonal[:, None, :]
    for sweep in range(ITERS):
        product = jnp.einsum("wij,wjk->wik", intersection, inverse, precision=lax.Precision.HIGHEST)
        inverse = jnp.einsum(
            "wij,wjk->wik",
            inverse,
            2.0 * identity[None, :, :] - product,
            precision=lax.Precision.HIGHEST,
        )
    theta = jnp.einsum("wnk,wkj->wnj", widened, inverse, precision=lax.Precision.HIGHEST)
    return theta.astype(jnp.bfloat16)


def block_energy(theta, vectors):
    blocks = jnp.einsum("gin,wnj->wgij", vectors, theta, preferred_element_type=jnp.float32)
    traces = jnp.einsum("wgii->wg", blocks)
    crossed = jnp.sum(blocks * jnp.swapaxes(blocks, 2, 3), axis=(2, 3))
    return 0.5 * jnp.sum(traces * traces - crossed, axis=1)


def swap_pairs(x, axis, size, bit):
    perm = [(i, i ^ bit) for i in range(size)]
    return lax.ppermute(x, axis, perm)


def body(old_walkers, half_chol, parent, field):
    n_walk = lax.axis_size("walk")
    old_dev = old_walkers.shape[0]
    slot_dev = parent.shape[0]
    walk_id = lax.axis_index("walk")
    core = walk_id % 2
    local_g = half_chol.shape[0]
    half_g = local_g // 2
    mine = lax.dynamic_slice_in_dim(half_chol, core * half_g, half_g, axis=0)
    gathered = lax.all_gather(mine, "chol", axis=0, tiled=True)
    other = swap_pairs(gathered, "walk", n_walk, 1)
    across = swap_pairs(old_walkers, "walk", n_walk, 2)
    beside = swap_pairs(old_walkers, "walk", n_walk, 1)
    diagonal_peer = swap_pairs(across, "walk", n_walk, 1)
    column = jnp.concatenate([old_walkers, beside, across, diagonal_peer], axis=0)
    living = parent >= 0
    source = jnp.maximum(parent, 0)
    relative = source // old_dev ^ walk_id
    index = relative * old_dev + source % old_dev
    kicked = (jnp.exp(field)[:, :, None] * column[index].astype(jnp.float32)).astype(jnp.bfloat16)
    new_walkers = jnp.where(living[:, None, None], kicked, jnp.zeros_like(kicked))
    theta = green_half(kicked)
    energy = block_energy(theta, gathered) + block_energy(theta, other)
    energy = jnp.where(living, energy, 0.0)
    return (new_walkers, energy)


def solution(mesh):
    return jax.shard_map(
        body,
        mesh=mesh,
        in_specs=(
            P(("walk", "chol"), None, None),
            P("chol", None, None),
            P(("walk", "chol")),
            P(("walk", "chol"), None),
        ),
        out_specs=(P(("walk", "chol"), None, None), P(("walk", "chol"))),
        check_vma=False,
    )
```

profile of v0, /device:TPU:1, one launch (start us, length us, event | category | flops | bytes accessed | tf_op | source)
XLA Modules:
  0.0 153.9 jit_solution(10622074899993358610)
XLA Ops:
  7.2 0.0 copy-start
  7.2 0.0 all-gather.2.cloned.1.call-start
  7.2 1.2 copy-done
  8.4 0.8 constant_dynamic-slice_fusion
  9.2 0.0 all-gather.2.cloned.1.call-update
  9.3 2.1 %collective-permute-start.1 = (bf16[3,2048,128]{2,1,0:T(8,128)(2,1)}, bf16[3,2048,128]{2,1,0:T(8,128)(2,1)S(1)}, u32[]{:S(2)}, u32[]{:S(2)}) collective-permute-start(bf16[3,2048,128]{2,1,0:T(8,128)(2,1)} %param.4), channel_id=1, source_target_pairs={{0,16},{8,24},{16,0},{24,8},{1,17},{9,25},{17,1},{25,9},{2,18},{10... | collective-permute-start | bytes 4718600 | tf_op jit(solution)/shard_map/ppermute | solution.py:37
  11.4 1.0 collective-permute-start
  12.3 33.4 %collective-permute-done.1 = bf16[3,2048,128]{2,1,0:T(8,128)(2,1)S(1)} collective-permute-done((bf16[3,2048,128]{2,1,0:T(8,128)(2,1)}, bf16[3,2048,128]{2,1,0:T(8,128)(2,1)S(1)}, u32[]{:S(2)}, u32[]{:S(2)}) %collective-permute-start.1) | collective-permute-done | bytes 1572896 | tf_op jit(solution)/shard_map/ppermute | solution.py:37
  45.7 1.2 collective-permute-start.2
  46.9 0.9 exp.3
  47.8 0.7 compare_select_fusion
  48.6 0.7 broadcast_compare_fusion
  49.2 35.8 %all-gather.2.cloned.1.call-done = bf16[8,128,2048]{2,1,0:T(8,128)(2,1)} async-done(((bf16[1,128,2048]{2,1,0:T(8,128)(2,1)}), bf16[8,128,2048]{2,1,0:T(8,128)(2,1)}) %all-gather.2.cloned.1.call-update) | async-done | bytes 4194320 | tf_op jit(solution)/shard_map/all_gather | solution.py:49
  85.0 1.9 %collective-permute-start.3 = (bf16[8,128,2048]{2,1,0:T(8,128)(2,1)}, bf16[8,128,2048]{2,1,0:T(8,128)(2,1)}, u32[]{:S(2)}, u32[]{:S(2)}) collective-permute-start(bf16[8,128,2048]{2,1,0:T(8,128)(2,1)} %all-gather.2.cloned.1.call-done), channel_id=1, source_target_pairs={{0,8},{8,0},{16,24},{24,16},{1,9},{9,1},{17,25},{25,17},{2,10},{10... | collective-permute-start | bytes 12582920 | tf_op jit(solution)/shard_map/ppermute | solution.py:37
  86.9 0.0 collective-permute-done
  86.9 0.0 collective-permute-done.2
  86.9 5.8 %pad_maximum_fusion = bf16[12,2048,128]{2,1,0:T(8,128)(2,1)} fusion(bf16[3,2048,128]{2,1,0:T(8,128)(2,1)} %collective-permute-done.2, bf16[3,2048,128]{2,1,0:T(8,128)(2,1)S(1)} %collective-permute-done.1, bf16[3,2048,128]{2,1,0:T(8,128)(2,1)} %collective-permute-done, bf16[3,2048,128]{2,1,0:T(8,128)(2,1)} %param.4), kind=kLoop, calls=%fused_computation.2 | loop fusion | flops 9437184 | bytes 12582912 | tf_op jit(solution)/shard_map/concatenate | solution.py:54
  92.7 5.5 %gather_fusion = bf16[6,2048,128]{2,1,0:T(8,128)(2,1)} fusion(bf16[12,2048,128]{2,1,0:T(8,128)(2,1)} %pad_maximum_fusion, s32[1024]{0:T(1024)S(1)} %pad_clamp_fusion), kind=kCustom, calls=%fused_computation | custom fusion | bytes 6291480 | tf_op jit(solution)/shard_map/gather | solution.py:59
  98.2 5.1 %broadcast_select_fusion = (bf16[6,2048,128]{2,1,0:T(8,128)(2,1)}, bf16[6,2048,128]{2,1,0:T(8,128)(2,1)S(1)}) fusion(pred[6]{0:T(512)(128)(4,1)S(1)} %broadcast_compare_fusion, bf16[6,2048,128]{2,1,0:T(8,128)(2,1)} %gather_fusion, f32[6,2048]{1,0:T(8,128)S(1)} %exp.3), kind=kLoop, calls=%fused_computation.19 | loop fusion | flops 6291456 | bytes 9486342 | tf_op jit(solution)/shard_map/jit(_where)/select_n | solution.py:60
  103.3 0.0 copy-start.1
  103.3 1.7 %copy-done.1 = bf16[6,2048,128]{2,1,0:T(8,128)(2,1)} copy-done((bf16[6,2048,128]{2,1,0:T(8,128)(2,1)}, bf16[6,2048,128]{2,1,0:T(8,128)(2,1)S(1)}, u32[]{:S(2)}) %copy-start.1) | copy-done | bytes 3145752
  105.0 4.7 %copy.26 = f32[6,128,128]{0,2,1:T(8,128)} copy(f32[6,128,128]{2,1,0:T(8,128)S(1)} %slice_convert_fusion) | data formatting | bytes 786432 | tf_op jit(solution)/shard_map/slice | solution.py:12
  109.7 1.8 %gather_fusion.1 = f32[128,6]{1,0:T(8,128)S(1)} fusion(f32[6,128,128]{0,2,1:T(8,128)} %copy.26, s32[128]{0:T(128)S(1)} %or_bitcast_fusion), kind=kCustom, calls=%fused_computation.1 | custom fusion | bytes 7168 | tf_op jit(solution)/shard_map/jit(diagonal)/gather | solution.py:14
  111.5 0.1 copy.27
  111.6 0.0 copy-start.2
  111.6 1.5 convolution_subtract_fusion.2
  113.0 0.5 fusion.10
  113.6 1.3 convolution_subtract_fusion.1
  114.9 0.5 fusion.23
  115.4 0.0 copy-done.2
  115.4 0.3 convolution_subtract_fusion
  115.8 0.5 fusion.24
  116.3 0.0 copy-start.5
  116.3 2.8 %convolution_convert_fusion = bf16[6,2048,128]{2,1,0:T(8,128)(2,1)S(1)} fusion(bf16[6,2048,128]{2,1,0:T(8,128)(2,1)S(1)} %copy-done.2, f32[6,128,128]{2,1,0:T(8,128)S(1)} %fusion.24), kind=kOutput, calls=%fused_computation.8 | convolution fusion | flops 2417491968 | bytes 6684672 | tf_op jit(solution)/shard_map/wnk,wkj->wnj/dot_general | solution.py:24
  119.1 0.0 copy-start.3
  119.1 1.7 %copy-done.3 = bf16[6,2048,128]{2,1,0:T(8,128)(2,1)} copy-done((bf16[6,2048,128]{2,1,0:T(8,128)(2,1)}, bf16[6,2048,128]{2,1,0:T(8,128)(2,1)S(1)}, u32[]{:S(2)}) %copy-start.3) | copy-done | bytes 3145752
  120.8 0.0 copy-done.5
  120.8 5.1 %fusion.2 = f32[6,128,8,128]{3,1,2,0:T(8,128)} fusion(bf16[8,128,2048]{2,1,0:T(8,128)(2,1)S(1)} %copy-done.5, bf16[6,2048,128]{2,1,0:T(8,128)(2,1)S(1)} %convolution_convert_fusion), kind=kOutput, calls=%fused_computation.6 | convolution fusion | flops 3221225472 | bytes 10485760 | tf_op jit(solution)/shard_map/gin,wnj->wgij/dot_general | solution.py:29
  125.9 3.6 %copy.29 = f32[6,128,8,128]{1,3,2,0:T(8,128)} copy(f32[6,128,8,128]{3,1,2,0:T(8,128)} %fusion.2) | data formatting | bytes 6291456 | tf_op jit(solution)/shard_map/gin,wnj->wgij/dot_general | solution.py:29
  129.5 0.0 collective-permute-done.3
  129.5 7.4 %fusion = f32[6,128,8,128]{3,1,2,0:T(8,128)} fusion(bf16[8,128,2048]{2,1,0:T(8,128)(2,1)} %collective-permute-done.3, bf16[6,2048,128]{2,1,0:T(8,128)(2,1)} %copy-done.3), kind=kOutput, calls=%fused_computation.4 | convolution fusion | flops 3221225472 | bytes 10485760 | tf_op jit(solution)/shard_map/gin,wnj->wgij/dot_general | solution.py:29
  136.9 3.5 %copy.31 = f32[6,128,8,128]{1,3,2,0:T(8,128)} copy(f32[6,128,8,128]{3,1,2,0:T(8,128)} %fusion) | data formatting | bytes 6291456 | tf_op jit(solution)/shard_map/gin,wnj->wgij/dot_general | solution.py:29
  140.4 0.0 copy-start.4
  140.4 5.9 %fusion.7 = (f32[6,8]{1,0:T(8,128)S(1)}, f32[6,8]{1,0:T(8,128)S(1)}, f32[6,8]{1,0:T(8,128)S(1)}, f32[6,8]{1,0:T(8,128)S(1)}) fusion(f32[6,128,8,128]{1,3,2,0:T(8,128)} %copy.31, pred[128,128]{1,0:T(8,128)(4,1)S(1)} %iota_compare_fusion.1, f32[6,128,8,128]{3,1,2,0:T(8,128)} %fusion, f32[6,128,8,128]{3,1,2,0:T(8,128)} %fusion.2, f32[6,128,8,128]{1,3,2,0:T(8,128)} %copy.29), kind=kLoop, calls=%fused_computation.14 | loop fusion | flops 6291264 | bytes 12600064 | tf_op jit(solution)/shard_map/wgii->wg/reduce_sum | solution.py:30
  146.3 0.1 subtract_reduce_fusion
  146.5 0.0 copy-done.4
  146.5 0.5 multiply_select_fusion
  (6 shorter events, 0.1 us)
Async XLA Ops:
  7.2 1.2 copy-start
  7.2 77.9 %all-gather.2.cloned.1.call-start = ((), (), s32[]{:S(2)}) async-start(), calls=%async_computation | async-start | bytes 4718592 | tf_op jit(solution)/shard_map/all_gather | solution.py:49
  9.3 36.4 %collective-permute-start.1 = (bf16[3,2048,128]{2,1,0:T(8,128)(2,1)}, bf16[3,2048,128]{2,1,0:T(8,128)(2,1)S(1)}, u32[]{:S(2)}, u32[]{:S(2)}) collective-permute-start(bf16[3,2048,128]{2,1,0:T(8,128)(2,1)} %param.4), channel_id=1, source_target_pairs={{0,16},{8,24},{16,0},{24,8},{1,17},{9,25},{17,1},{25,9},{2,18},{10... | collective-permute-start | bytes 4718600 | tf_op jit(solution)/shard_map/ppermute | solution.py:37
  11.4 75.5 %collective-permute-start = (bf16[3,2048,128]{2,1,0:T(8,128)(2,1)}, bf16[3,2048,128]{2,1,0:T(8,128)(2,1)}, u32[]{:S(2)}, u32[]{:S(2)}) collective-permute-start(bf16[3,2048,128]{2,1,0:T(8,128)(2,1)} %param.4), channel_id=1, source_target_pairs={{0,8},{8,0},{16,24},{24,16},{1,9},{9,1},{17,25},{25,17},{2,10},{10... | collective-permute-start | bytes 4718600 | tf_op jit(solution)/shard_map/ppermute | solution.py:37
  45.7 41.2 %collective-permute-start.2 = (bf16[3,2048,128]{2,1,0:T(8,128)(2,1)S(1)}, bf16[3,2048,128]{2,1,0:T(8,128)(2,1)}, u32[]{:S(2)}, u32[]{:S(2)}) collective-permute-start(bf16[3,2048,128]{2,1,0:T(8,128)(2,1)S(1)} %collective-permute-done.1), channel_id=1, source_target_pairs={{0,8},{8,0},{16,24},{24,16},{1,9},{9,1},{17,25},{25,17},{2,10},{10... | collective-permute-start | bytes 4718600 | tf_op jit(solution)/shard_map/ppermute | solution.py:37
  85.0 44.5 %collective-permute-start.3 = (bf16[8,128,2048]{2,1,0:T(8,128)(2,1)}, bf16[8,128,2048]{2,1,0:T(8,128)(2,1)}, u32[]{:S(2)}, u32[]{:S(2)}) collective-permute-start(bf16[8,128,2048]{2,1,0:T(8,128)(2,1)} %all-gather.2.cloned.1.call-done), channel_id=1, source_target_pairs={{0,8},{8,0},{16,24},{24,16},{1,9},{9,1},{17,25},{25,17},{2,10},{10... | collective-permute-start | bytes 12582920 | tf_op jit(solution)/shard_map/ppermute | solution.py:37
  103.3 1.7 %copy-start.1 = (bf16[6,2048,128]{2,1,0:T(8,128)(2,1)}, bf16[6,2048,128]{2,1,0:T(8,128)(2,1)S(1)}, u32[]{:S(2)}) copy-start(bf16[6,2048,128]{2,1,0:T(8,128)(2,1)S(1)} %get-tuple-element.11) | copy-start | bytes 9437188
  111.6 3.9 %copy-start.2 = (bf16[6,2048,128]{2,1,0:T(8,128)(2,1)S(1)}, bf16[6,2048,128]{2,1,0:T(8,128)(2,1)}, u32[]{:S(2)}) copy-start(bf16[6,2048,128]{2,1,0:T(8,128)(2,1)} %copy-done.1) | copy-start | bytes 9437188
  116.3 4.5 %copy-start.5 = (bf16[8,128,2048]{2,1,0:T(8,128)(2,1)S(1)}, bf16[8,128,2048]{2,1,0:T(8,128)(2,1)}, u32[]{:S(2)}) copy-start(bf16[8,128,2048]{2,1,0:T(8,128)(2,1)} %all-gather.2.cloned.1.call-done) | copy-start | bytes 12582916
  119.1 1.7 %copy-start.3 = (bf16[6,2048,128]{2,1,0:T(8,128)(2,1)}, bf16[6,2048,128]{2,1,0:T(8,128)(2,1)S(1)}, u32[]{:S(2)}) copy-start(bf16[6,2048,128]{2,1,0:T(8,128)(2,1)S(1)} %convolution_convert_fusion) | copy-start | bytes 9437188
  140.4 6.1 %copy-start.4 = (s32[6]{0:T(128)S(1)}, s32[6]{0:T(128)}, u32[]{:S(2)}) copy-start(s32[6]{0:T(128)} %param.6) | copy-start | bytes 76
Sparse Core Ops, SparseCore 0:
  10.7 74.2 all-gather.1
where the time goes:
time: 154 us
  waiting for transfers between devices  69.2 us (45%)
  local copies, waits for them, and re-layouts  25.4 us (16%)
  matrix products  20 us (13%)
  other arithmetic  18.9 us (12%)
  between operations  14.2 us (9%)
  starting transfers between devices  6.19 us (4%)
    all_gather x1, waiting for transfers between devices, body(): gathered = lax.all_gather(mine, 'chol', axis=0, tiled=True)  35.8 us
    ppermute x4, waiting for transfers between devices, swap_pairs(): return lax.ppermute(x, axis, perm)  33.4 us
    dot_general x2, matrix products, block_energy(): jnp.einsum('gin,wnj->wgij', vectors, theta, preferred_element_type=jnp.fl...  12.5 us
    dot_general x2, local copies, waits for them, and re-layouts, block_energy(): jnp.einsum('gin,wnj->wgij', vectors, theta, preferred_element_type=jnp.fl...  7.09 us
    ppermute x4, starting transfers between devices, swap_pairs(): return lax.ppermute(x, axis, perm)  6.15 us
    reduce_sum x1, other arithmetic, block_energy(): traces = jnp.einsum('wgii->wg', blocks)  5.93 us
    concatenate x1, other arithmetic, body(): jnp.concatenate([old_walkers, beside, across, diagonal_peer], axis=0)  5.83 us
    gather x1, local copies, waits for them, and re-layouts, body(): column[index].astype(jnp.float32)  5.5 us
  transfers between devices with their start and end apart: 5, of which 2 were waited for; matrix products, arithmetic and copies ran while one was open for 27% of the time, Pallas kernels for 0%

commit v1 on v0

--- a/solution.py
+++ b/solution.py
@@ -46,7 +46,14 @@
     local_g = half_chol.shape[0]
     half_g = local_g // 2
     mine = lax.dynamic_slice_in_dim(half_chol, core * half_g, half_g, axis=0)
-    gathered = lax.all_gather(mine, "chol", axis=0, tiled=True)
+    count = lax.axis_size("chol")
+    right = [(i_2, (i_2 + 1) % count) for i_2 in range(count)]
+    pieces = [mine]
+    for reach in range(1, count):
+        pieces = [lax.ppermute(pieces[0], "chol", right), *pieces]
+    result = jnp.concatenate(pieces, axis=0)
+    shift = (lax.axis_index("chol") + 1) * pieces[-1].shape[0]
+    gathered = jnp.roll(result, shift, axis=0)
     other = swap_pairs(gathered, "walk", n_walk, 1)
     across = swap_pairs(old_walkers, "walk", n_walk, 2)
     beside = swap_pairs(old_walkers, "walk", n_walk, 1)

time: 154 us -> 168 us (1.091)
  between operations: 14.2 us -> 0.91 us
  starting transfers between devices: 6.19 us -> 17 us
  waiting for transfers between devices: 69.2 us -> 79.3 us
  local copies, waits for them, and re-layouts: 25.4 us -> 28.9 us
  matrix products: 20 us -> 21.7 us
    ppermute x0 -> x7, waiting for transfers between devices: none -> 72.7 us  [body(): pieces = [lax.ppermute(pieces[0], 'chol', right), *pieces]]
    all_gather x1 -> x0, waiting for transfers between devices: 35.8 us -> none  [body(): gathered = lax.all_gather(mine, 'chol', axis=0, tiled=True)]
    ppermute x4, waiting for transfers between devices: 33.4 us -> 6.54 us  [swap_pairs(): return lax.ppermute(x, axis, perm)]
    ppermute x4, starting transfers between devices: 6.15 us -> 14.9 us  [swap_pairs(): return lax.ppermute(x, axis, perm)]
    dynamic_slice x0 -> x1, local copies, waits for them, and re-layouts: none -> 2.29 us  [body(): gathered = jnp.roll(result, shift, axis=0)]
    ppermute x0 -> x7, starting transfers between devices: none -> 2.14 us  [body(): pieces = [lax.ppermute(pieces[0], 'chol', right), *pieces]]
    unnamed x12 -> x25, local copies, waits for them, and re-layouts: 4.49 us -> 6.47 us
  transfers between devices with their start and end apart: 5 -> 11, of which waited for: 2 -> 7; matrix products, arithmetic and copies ran while one was open for 27% -> 30% of each run, Pallas kernels for 0% -> 0%
where the time goes in v1:
time: 168 us; the launch traced here: 167 us
  waiting for transfers between devices  79.3 us (47%)
  local copies, waits for them, and re-layouts  28.9 us (17%)
  matrix products  21.7 us (13%)
  other arithmetic  19.3 us (11%)
  starting transfers between devices  17 us (10%)
    ppermute x7, waiting for transfers between devices, body(): pieces = [lax.ppermute(pieces[0], 'chol', right), *pieces]  72.7 us
    ppermute x4, starting transfers between devices, swap_pairs(): return lax.ppermute(x, axis, perm)  14.9 us
    dot_general x2, matrix products, block_energy(): jnp.einsum('gin,wnj->wgij', vectors, theta, preferred_element_type=jnp.fl...  12.8 us
    ppermute x4, waiting for transfers between devices, swap_pairs(): return lax.ppermute(x, axis, perm)  6.54 us
    unnamed x25, local copies, waits for them, and re-layouts  6.47 us
    dot_general x2, local copies, waits for them, and re-layouts, block_energy(): jnp.einsum('gin,wnj->wgij', vectors, theta, preferred_element_type=jnp.fl...  5.99 us
    gather x1, local copies, waits for them, and re-layouts, body(): column[index].astype(jnp.float32)  5.5 us
    concatenate x1, other arithmetic, body(): jnp.concatenate([old_walkers, beside, across, diagonal_peer], axis=0)  5.29 us
  transfers between devices with their start and end apart: 11, of which 7 were waited for; matrix products, arithmetic and copies ran while one was open for 30% of the time, Pallas kernels for 0%

profile of v1, /device:TPU:1, one launch (start us, length us, event | category | flops | bytes accessed | tf_op | source)
XLA Modules:
  0.0 167.0 jit_solution(15794823494766441189)
XLA Ops:
  0.7 1.2 constant_dynamic-slice_fusion.1
  1.8 2.1 %collective-permute-start.3 = (bf16[1,128,2048]{2,1,0:T(8,128)(2,1)S(1)}, bf16[1,128,2048]{2,1,0:T(8,128)(2,1)S(1)}, u32[]{:S(2)}, u32[]{:S(2)}) collective-permute-start(bf16[1,128,2048]{2,1,0:T(8,128)(2,1)S(1)} %constant_dynamic-slice_fusion.1), channel_id=1, source_target_pairs={{0,1},{1,2},{2,3},{3,4},{4,5},{5,6},{6,7},{7,0},{8,9},{9,10},{10,1... | collective-permute-start | bytes 1572872 | tf_op jit(solution)/shard_map/ppermute | solution.py:53
  3.9 14.7 %collective-permute-done.3 = bf16[1,128,2048]{2,1,0:T(8,128)(2,1)S(1)} collective-permute-done((bf16[1,128,2048]{2,1,0:T(8,128)(2,1)S(1)}, bf16[1,128,2048]{2,1,0:T(8,128)(2,1)S(1)}, u32[]{:S(2)}, u32[]{:S(2)}) %collective-permute-start.3) | collective-permute-done | bytes 524320 | tf_op jit(solution)/shard_map/ppermute | solution.py:53
  18.6 0.0 collective-permute-start.4
  18.6 14.9 %collective-permute-done.4 = bf16[1,128,2048]{2,1,0:T(8,128)(2,1)S(1)} collective-permute-done((bf16[1,128,2048]{2,1,0:T(8,128)(2,1)S(1)}, bf16[1,128,2048]{2,1,0:T(8,128)(2,1)S(1)}, u32[]{:S(2)}, u32[]{:S(2)}) %collective-permute-start.4) | collective-permute-done | bytes 524320 | tf_op jit(solution)/shard_map/ppermute | solution.py:53
  33.5 0.0 collective-permute-start.5
  33.5 14.0 %collective-permute-done.5 = bf16[1,128,2048]{2,1,0:T(8,128)(2,1)S(1)} collective-permute-done((bf16[1,128,2048]{2,1,0:T(8,128)(2,1)S(1)}, bf16[1,128,2048]{2,1,0:T(8,128)(2,1)S(1)}, u32[]{:S(2)}, u32[]{:S(2)}) %collective-permute-start.5) | collective-permute-done | bytes 524320 | tf_op jit(solution)/shard_map/ppermute | solution.py:53
  47.5 13.0 %collective-permute-done.6 = bf16[1,128,2048]{2,1,0:T(8,128)(2,1)S(1)} collective-permute-done((bf16[1,128,2048]{2,1,0:T(8,128)(2,1)S(1)}, bf16[1,128,2048]{2,1,0:T(8,128)(2,1)S(1)}, u32[]{:S(2)}, u32[]{:S(2)}) %collective-permute-start.6) | collective-permute-done | bytes 524320 | tf_op jit(solution)/shard_map/ppermute | solution.py:53
  60.5 0.5 collective-permute-start.1
  61.0 11.7 %collective-permute-done.7 = bf16[1,128,2048]{2,1,0:T(8,128)(2,1)} collective-permute-done((bf16[1,128,2048]{2,1,0:T(8,128)(2,1)S(1)}, bf16[1,128,2048]{2,1,0:T(8,128)(2,1)}, u32[]{:S(2)}, u32[]{:S(2)}) %collective-permute-start.7) | collective-permute-done | bytes 524320 | tf_op jit(solution)/shard_map/ppermute | solution.py:53
  72.8 4.9 %collective-permute-start = (bf16[3,2048,128]{2,1,0:T(8,128)(2,1)}, bf16[3,2048,128]{2,1,0:T(8,128)(2,1)}, u32[]{:S(2)}, u32[]{:S(2)}) collective-permute-start(bf16[3,2048,128]{2,1,0:T(8,128)(2,1)} %param.4), channel_id=1, source_target_pairs={{0,8},{8,0},{16,24},{24,16},{1,9},{9,1},{17,25},{25,17},{2,10},{10... | collective-permute-start | bytes 4718600 | tf_op jit(solution)/shard_map/ppermute | solution.py:37
  77.7 0.9 exp.3
  78.5 0.7 compare_select_fusion
  79.2 0.6 iota_compare_fusion.1
  79.8 4.4 %collective-permute-done.8 = bf16[1,128,2048]{2,1,0:T(8,128)(2,1)} collective-permute-done((bf16[1,128,2048]{2,1,0:T(8,128)(2,1)}, bf16[1,128,2048]{2,1,0:T(8,128)(2,1)}, u32[]{:S(2)}, u32[]{:S(2)}) %collective-permute-start.8) | collective-permute-done | bytes 524320 | tf_op jit(solution)/shard_map/ppermute | solution.py:53
  84.3 0.6 fusion.20
  84.9 0.6 fusion.21
  85.5 0.7 broadcast_compare_fusion
  86.2 6.5 %collective-permute-done.1 = bf16[3,2048,128]{2,1,0:T(8,128)(2,1)} collective-permute-done((bf16[3,2048,128]{2,1,0:T(8,128)(2,1)}, bf16[3,2048,128]{2,1,0:T(8,128)(2,1)}, u32[]{:S(2)}, u32[]{:S(2)}) %collective-permute-start.1) | collective-permute-done | bytes 1572896 | tf_op jit(solution)/shard_map/ppermute | solution.py:37
  92.7 4.9 %collective-permute-start.2 = (bf16[3,2048,128]{2,1,0:T(8,128)(2,1)}, bf16[3,2048,128]{2,1,0:T(8,128)(2,1)S(1)}, u32[]{:S(2)}, u32[]{:S(2)}) collective-permute-start(bf16[3,2048,128]{2,1,0:T(8,128)(2,1)} %collective-permute-done.1), channel_id=1, source_target_pairs={{0,8},{8,0},{16,24},{24,16},{1,9},{9,1},{17,25},{25,17},{2,10},{10... | collective-permute-start | bytes 4718600 | tf_op jit(solution)/shard_map/ppermute | solution.py:37
  97.7 1.1 constant_dynamic-update-slice_fusion.14
  98.8 1.1 constant_dynamic-update-slice_fusion.13
  100.2 1.1 constant_dynamic-update-slice_fusion.6
  101.2 1.1 constant_dynamic-update-slice_fusion.5
  102.4 0.0 copy-start.2
  102.6 2.3 %constant_dynamic-slice_fusion = bf16[8,128,2048]{2,1,0:T(8,128)(2,1)} fusion(bf16[16,128,2048]{2,1,0:T(8,128)(2,1)S(1)} %constant_dynamic-update-slice_fusion, s32[]{:T(128)S(6)} %select_n.61), kind=kLoop, calls=%fused_computation.63 | loop fusion | bytes 8388612 | tf_op jit(solution)/shard_map/jit(_roll_dynamic)/dynamic_slice | solution.py:56
  104.9 4.5 %collective-permute-start.10 = (bf16[8,128,2048]{2,1,0:T(8,128)(2,1)}, bf16[8,128,2048]{2,1,0:T(8,128)(2,1)}, u32[]{:S(2)}, u32[]{:S(2)}) collective-permute-start(bf16[8,128,2048]{2,1,0:T(8,128)(2,1)} %constant_dynamic-slice_fusion), channel_id=1, source_target_pairs={{0,8},{8,0},{16,24},{24,16},{1,9},{9,1},{17,25},{25,17},{2,10},{10... | collective-permute-start | bytes 12582920 | tf_op jit(solution)/shard_map/ppermute | solution.py:37
  109.4 5.3 %pad_maximum_fusion = bf16[12,2048,128]{2,1,0:T(8,128)(2,1)} fusion(bf16[3,2048,128]{2,1,0:T(8,128)(2,1)S(1)} %collective-permute-done.2, bf16[3,2048,128]{2,1,0:T(8,128)(2,1)} %collective-permute-done.1, bf16[3,2048,128]{2,1,0:T(8,128)(2,1)} %collective-permute-done, bf16[3,2048,128]{2,1,0:T(8,128)(2,1)S(1)} %copy-done.2), kind=kLoop, calls=%fused_computation.2 | loop fusion | flops 9437184 | bytes 12582912 | tf_op jit(solution)/shard_map/concatenate | solution.py:61
  114.7 5.5 %gather_fusion = bf16[6,2048,128]{2,1,0:T(8,128)(2,1)} fusion(bf16[12,2048,128]{2,1,0:T(8,128)(2,1)} %pad_maximum_fusion, s32[1024]{0:T(1024)S(1)} %pad_clamp_fusion), kind=kCustom, calls=%fused_computation | custom fusion | bytes 6291480 | tf_op jit(solution)/shard_map/gather | solution.py:66
  120.2 5.1 %broadcast_select_fusion = (bf16[6,2048,128]{2,1,0:T(8,128)(2,1)}, bf16[6,2048,128]{2,1,0:T(8,128)(2,1)S(1)}) fusion(pred[6]{0:T(512)(128)(4,1)S(1)} %broadcast_compare_fusion, bf16[6,2048,128]{2,1,0:T(8,128)(2,1)} %gather_fusion, f32[6,2048]{1,0:T(8,128)S(1)} %exp.3), kind=kLoop, calls=%fused_computation.19 | loop fusion | flops 6291456 | bytes 9486342 | tf_op jit(solution)/shard_map/jit(_where)/select_n | solution.py:67
  125.3 4.7 %copy.20 = f32[6,128,128]{0,2,1:T(8,128)} copy(f32[6,128,128]{2,1,0:T(8,128)S(1)} %slice_convert_fusion) | data formatting | bytes 786432 | tf_op jit(solution)/shard_map/slice | solution.py:12
  130.0 1.8 %gather_fusion.1 = f32[128,6]{1,0:T(8,128)S(1)} fusion(f32[6,128,128]{0,2,1:T(8,128)} %copy.20, s32[128]{0:T(128)S(1)} %or_bitcast_fusion), kind=kCustom, calls=%fused_computation.1 | custom fusion | bytes 7168 | tf_op jit(solution)/shard_map/jit(diagonal)/gather | solution.py:14
  131.8 0.1 copy.21
  131.8 1.3 convolution_subtract_fusion.2
  133.1 1.4 fusion.10
  134.5 1.2 convolution_subtract_fusion.1
  135.7 0.5 fusion.23
  136.2 1.2 convolution_subtract_fusion
  137.4 0.5 fusion.24
  137.9 2.8 %convolution_convert_fusion = bf16[6,2048,128]{2,1,0:T(8,128)(2,1)S(1)} fusion(bf16[6,2048,128]{2,1,0:T(8,128)(2,1)S(1)} %get-tuple-element.11, f32[6,128,128]{2,1,0:T(8,128)S(1)} %fusion.24), kind=kOutput, calls=%fused_computation.8 | convolution fusion | flops 2417491968 | bytes 6684672 | tf_op jit(solution)/shard_map/wnk,wkj->wnj/dot_general | solution.py:24
  140.8 1.7 %copy-done = bf16[6,2048,128]{2,1,0:T(8,128)(2,1)} copy-done((bf16[6,2048,128]{2,1,0:T(8,128)(2,1)}, bf16[6,2048,128]{2,1,0:T(8,128)(2,1)S(1)}, u32[]{:S(2)}) %copy-start) | copy-done | bytes 3145752
  142.5 5.3 %fusion.2 = f32[6,128,8,128]{3,1,2,0:T(8,128)S(1)} fusion(bf16[8,128,2048]{2,1,0:T(8,128)(2,1)} %constant_dynamic-slice_fusion, bf16[6,2048,128]{2,1,0:T(8,128)(2,1)S(1)} %convolution_convert_fusion), kind=kOutput, calls=%fused_computation.6 | convolution fusion | flops 3221225472 | bytes 10485760 | tf_op jit(solution)/shard_map/gin,wnj->wgij/dot_general | solution.py:29
  147.8 2.4 %copy.23 = f32[6,128,8,128]{1,3,2,0:T(8,128)} copy(f32[6,128,8,128]{3,1,2,0:T(8,128)S(1)} %fusion.2) | data formatting | bytes 6291456 | tf_op jit(solution)/shard_map/gin,wnj->wgij/dot_general | solution.py:29
  150.3 7.5 %fusion = f32[6,128,8,128]{3,1,2,0:T(8,128)} fusion(bf16[8,128,2048]{2,1,0:T(8,128)(2,1)} %collective-permute-done.10, bf16[6,2048,128]{2,1,0:T(8,128)(2,1)} %copy-done), kind=kOutput, calls=%fused_computation.4 | convolution fusion | flops 3221225472 | bytes 10485760 | tf_op jit(solution)/shard_map/gin,wnj->wgij/dot_general | solution.py:29
  157.7 3.5 %copy.25 = f32[6,128,8,128]{1,3,2,0:T(8,128)} copy(f32[6,128,8,128]{3,1,2,0:T(8,128)} %fusion) | data formatting | bytes 6291456 | tf_op jit(solution)/shard_map/gin,wnj->wgij/dot_general | solution.py:29
  161.3 5.0 %fusion.7 = (f32[6,8]{1,0:T(8,128)S(1)}, f32[6,8]{1,0:T(8,128)S(1)}, f32[6,8]{1,0:T(8,128)S(1)}, f32[6,8]{1,0:T(8,128)S(1)}) fusion(f32[6,128,8,128]{1,3,2,0:T(8,128)} %copy.25, pred[128,128]{1,0:T(8,128)(4,1)S(1)} %copy-done.3, f32[6,128,8,128]{3,1,2,0:T(8,128)} %fusion, f32[6,128,8,128]{3,1,2,0:T(8,128)S(1)} %fusion.2, f32[6,128,8,128]{1,3,2,0:T(8,128)} %copy.23), kind=kLoop, calls=%fused_computation.14 | loop fusion | flops 6291264 | bytes 12600064 | tf_op jit(solution)/shard_map/wgii->wg/reduce_sum | solution.py:30
  166.3 0.1 subtract_reduce_fusion
  166.5 0.5 multiply_select_fusion
  (31 shorter events, 0.5 us)
Async XLA Ops:
  0.6 99.4 %copy-start.1 = (bf16[2,128,2048]{2,1,0:T(8,128)(2,1)S(1)}, bf16[2,128,2048]{2,1,0:T(8,128)(2,1)}, u32[]{:S(2)}) copy-start(bf16[2,128,2048]{2,1,0:T(8,128)(2,1)} %param.5) | copy-start | bytes 3145732
  1.8 16.8 %collective-permute-start.3 = (bf16[1,128,2048]{2,1,0:T(8,128)(2,1)S(1)}, bf16[1,128,2048]{2,1,0:T(8,128)(2,1)S(1)}, u32[]{:S(2)}, u32[]{:S(2)}) collective-permute-start(bf16[1,128,2048]{2,1,0:T(8,128)(2,1)S(1)} %constant_dynamic-slice_fusion.1), channel_id=1, source_target_pairs={{0,1},{1,2},{2,3},{3,4},{4,5},{5,6},{6,7},{7,0},{8,9},{9,10},{10,1... | collective-permute-start | bytes 1572872 | tf_op jit(solution)/shard_map/ppermute | solution.py:53
  18.6 14.9 %collective-permute-start.4 = (bf16[1,128,2048]{2,1,0:T(8,128)(2,1)S(1)}, bf16[1,128,2048]{2,1,0:T(8,128)(2,1)S(1)}, u32[]{:S(2)}, u32[]{:S(2)}) collective-permute-start(bf16[1,128,2048]{2,1,0:T(8,128)(2,1)S(1)} %collective-permute-done.3), channel_id=1, source_target_pairs={{0,1},{1,2},{2,3},{3,4},{4,5},{5,6},{6,7},{7,0},{8,9},{9,10},{10,1... | collective-permute-start | bytes 1572872 | tf_op jit(solution)/shard_map/ppermute | solution.py:53
  33.5 14.0 %collective-permute-start.5 = (bf16[1,128,2048]{2,1,0:T(8,128)(2,1)S(1)}, bf16[1,128,2048]{2,1,0:T(8,128)(2,1)S(1)}, u32[]{:S(2)}, u32[]{:S(2)}) collective-permute-start(bf16[1,128,2048]{2,1,0:T(8,128)(2,1)S(1)} %collective-permute-done.4), channel_id=1, source_target_pairs={{0,1},{1,2},{2,3},{3,4},{4,5},{5,6},{6,7},{7,0},{8,9},{9,10},{10,1... | collective-permute-start | bytes 1572872 | tf_op jit(solution)/shard_map/ppermute | solution.py:53
  47.5 13.0 %collective-permute-start.6 = (bf16[1,128,2048]{2,1,0:T(8,128)(2,1)S(1)}, bf16[1,128,2048]{2,1,0:T(8,128)(2,1)S(1)}, u32[]{:S(2)}, u32[]{:S(2)}) collective-permute-start(bf16[1,128,2048]{2,1,0:T(8,128)(2,1)S(1)} %collective-permute-done.5), channel_id=1, source_target_pairs={{0,1},{1,2},{2,3},{3,4},{4,5},{5,6},{6,7},{7,0},{8,9},{9,10},{10,1... | collective-permute-start | bytes 1572872 | tf_op jit(solution)/shard_map/ppermute | solution.py:53
  60.5 12.2 %collective-permute-start.7 = (bf16[1,128,2048]{2,1,0:T(8,128)(2,1)S(1)}, bf16[1,128,2048]{2,1,0:T(8,128)(2,1)}, u32[]{:S(2)}, u32[]{:S(2)}) collective-permute-start(bf16[1,128,2048]{2,1,0:T(8,128)(2,1)S(1)} %collective-permute-done.6), channel_id=1, source_target_pairs={{0,1},{1,2},{2,3},{3,4},{4,5},{5,6},{6,7},{7,0},{8,9},{9,10},{10,1... | collective-permute-start | bytes 1572872 | tf_op jit(solution)/shard_map/ppermute | solution.py:53
  60.5 32.2 %collective-permute-start.1 = (bf16[3,2048,128]{2,1,0:T(8,128)(2,1)}, bf16[3,2048,128]{2,1,0:T(8,128)(2,1)}, u32[]{:S(2)}, u32[]{:S(2)}) collective-permute-start(bf16[3,2048,128]{2,1,0:T(8,128)(2,1)} %param.4), channel_id=1, source_target_pairs={{0,16},{8,24},{16,0},{24,8},{1,17},{9,25},{17,1},{25,9},{2,18},{10... | collective-permute-start | bytes 4718600 | tf_op jit(solution)/shard_map/ppermute | solution.py:37
  72.8 11.5 %collective-permute-start.8 = (bf16[1,128,2048]{2,1,0:T(8,128)(2,1)}, bf16[1,128,2048]{2,1,0:T(8,128)(2,1)}, u32[]{:S(2)}, u32[]{:S(2)}) collective-permute-start(bf16[1,128,2048]{2,1,0:T(8,128)(2,1)} %collective-permute-done.7), channel_id=1, source_target_pairs={{0,1},{1,2},{2,3},{3,4},{4,5},{5,6},{6,7},{7,0},{8,9},{9,10},{10,1... | collective-permute-start | bytes 1572872 | tf_op jit(solution)/shard_map/ppermute | solution.py:53
  72.8 36.6 %collective-permute-start = (bf16[3,2048,128]{2,1,0:T(8,128)(2,1)}, bf16[3,2048,128]{2,1,0:T(8,128)(2,1)}, u32[]{:S(2)}, u32[]{:S(2)}) collective-permute-start(bf16[3,2048,128]{2,1,0:T(8,128)(2,1)} %param.4), channel_id=1, source_target_pairs={{0,8},{8,0},{16,24},{24,16},{1,9},{9,1},{17,25},{25,17},{2,10},{10... | collective-permute-start | bytes 4718600 | tf_op jit(solution)/shard_map/ppermute | solution.py:37
  84.3 13.4 %collective-permute-start.9 = (bf16[1,128,2048]{2,1,0:T(8,128)(2,1)}, bf16[1,128,2048]{2,1,0:T(8,128)(2,1)S(1)}, u32[]{:S(2)}, u32[]{:S(2)}) collective-permute-start(bf16[1,128,2048]{2,1,0:T(8,128)(2,1)} %collective-permute-done.8), channel_id=1, source_target_pairs={{0,1},{1,2},{2,3},{3,4},{4,5},{5,6},{6,7},{7,0},{8,9},{9,10},{10,1... | collective-permute-start | bytes 1572872 | tf_op jit(solution)/shard_map/ppermute | solution.py:53
  92.7 16.7 %collective-permute-start.2 = (bf16[3,2048,128]{2,1,0:T(8,128)(2,1)}, bf16[3,2048,128]{2,1,0:T(8,128)(2,1)S(1)}, u32[]{:S(2)}, u32[]{:S(2)}) collective-permute-start(bf16[3,2048,128]{2,1,0:T(8,128)(2,1)} %collective-permute-done.1), channel_id=1, source_target_pairs={{0,8},{8,0},{16,24},{24,16},{1,9},{9,1},{17,25},{25,17},{2,10},{10... | collective-permute-start | bytes 4718600 | tf_op jit(solution)/shard_map/ppermute | solution.py:37
  102.4 7.0 %copy-start.2 = (bf16[3,2048,128]{2,1,0:T(8,128)(2,1)S(1)}, bf16[3,2048,128]{2,1,0:T(8,128)(2,1)}, u32[]{:S(2)}) copy-start(bf16[3,2048,128]{2,1,0:T(8,128)(2,1)} %param.4) | copy-start | bytes 4718596
  104.9 45.4 %collective-permute-start.10 = (bf16[8,128,2048]{2,1,0:T(8,128)(2,1)}, bf16[8,128,2048]{2,1,0:T(8,128)(2,1)}, u32[]{:S(2)}, u32[]{:S(2)}) collective-permute-start(bf16[8,128,2048]{2,1,0:T(8,128)(2,1)} %constant_dynamic-slice_fusion), channel_id=1, source_target_pairs={{0,8},{8,0},{16,24},{24,16},{1,9},{9,1},{17,25},{25,17},{2,10},{10... | collective-permute-start | bytes 12582920 | tf_op jit(solution)/shard_map/ppermute | solution.py:37
  140.8 1.7 %copy-start = (bf16[6,2048,128]{2,1,0:T(8,128)(2,1)}, bf16[6,2048,128]{2,1,0:T(8,128)(2,1)S(1)}, u32[]{:S(2)}) copy-start(bf16[6,2048,128]{2,1,0:T(8,128)(2,1)S(1)} %convolution_convert_fusion) | copy-start | bytes 9437188
  157.7 3.5 %copy-start.3 = (pred[128,128]{1,0:T(8,128)(4,1)S(1)}, pred[128,128]{1,0:T(8,128)(4,1)}, u32[]{:S(2)}) copy-start(pred[128,128]{1,0:T(8,128)(4,1)} %iota_compare_fusion.1) | copy-start | bytes 49156
  161.3 5.2 %copy-start.4 = (s32[6]{0:T(128)S(1)}, s32[6]{0:T(128)}, u32[]{:S(2)}) copy-start(s32[6]{0:T(128)} %param.6) | copy-start | bytes 76
